TPU v7x, 256 devices: a whole 4x4x8 slice. The times are simulated.
256 devices in a mesh: blk: 64 (over y, x_lo, z), team: 4 (over x_hi, core).
Axes of the slice: x: 4 (x_hi: 2, x_lo: 2; x = x_hi * 2 + x_lo), y: 4, z: 8, core: 2. Of those that a mesh axis runs over, the one named last changes fastest.
Arguments:
- loadings: bfloat16 [64, 98304], P(None, ('blk', 'team')), may hold values from -6 to 6
- scales: bfloat16 [64, 768], P(None, ('blk', 'team')), may hold values from 0.25 to 4
- cov: bfloat16 [16384, 16, 4, 1536], P('blk', None, 'team'), may hold values from -0.01953125 to 0.01953125
Outputs:
- product: float32 [64, 16384], P(None, 'blk')
All inputs are finite; a program needn't handle non-finite values.
Results may differ from a plain program's by a relative error of at most 0.0028.
Values may be sent and summed in bfloat16 or wider, within the bound.
No kernel may reach another device: no remote copies, remote signals or barrier semaphores. Data moves between devices by JAX's collectives and lax.ppermute only.
A program may use at most 128 MiB of HBM per device.

v0:
```python
import jax
import jax.numpy as jnp
from jax import lax
from jax.sharding import PartitionSpec as P


def passed_along(x, axis, by):
    size = lax.axis_size(axis)
    return lax.ppermute(x, axis, [(i, (i + by) % size) for i in range(size)])


def per_device(loadings, scales, cov):
    team_size = lax.axis_size("team")
    cycle_size = lax.axis_size("blk")
    cycle_stops = cycle_size // team_size
    cycle_pos = lax.axis_index("blk")
    member = lax.axis_index("team")
    skew_lag = jnp.mod(cycle_pos - member, team_size)
    base_stop = jnp.mod((cycle_pos - skew_lag - member) // team_size, cycle_stops)
    held_block = (
        lax.all_gather(loadings, "team", axis=1, tiled=True),
        lax.all_gather(scales, "team", axis=1, tiled=True),
    )
    near_copy = passed_along((held_block[0], held_block[1]), "blk", 1)
    far_copies = passed_along((held_block[0], held_block[1], near_copy[0], near_copy[1]), "blk", 2)
    stacked_loads = jnp.stack([held_block[0], near_copy[0], far_copies[0], far_copies[2]])
    stacked_scales = jnp.stack([held_block[1], near_copy[1], far_copies[1], far_copies[3]])
    start_block = (
        lax.dynamic_index_in_dim(stacked_loads, skew_lag, 0, keepdims=False),
        lax.dynamic_index_in_dim(stacked_scales, skew_lag, 0, keepdims=False),
    )
    cov_local = cov[:, :, 0, :]
    n_loads = loadings.shape[0]
    row_count = cov.shape[0]

    def contribute(running, block, stop_num):
        block_load, block_scale = block
        groups = block_scale.shape[1]
        scaled = (
            (
                block_load.astype(jnp.float32).reshape(
                    n_loads, groups, block_load.shape[1] // groups
                )
                * block_scale.astype(jnp.float32)[:, :, None]
            )
            .reshape(n_loads, block_load.shape[1])
            .astype(jnp.bfloat16)
        )
        cov_slab = lax.dynamic_index_in_dim(
            cov_local, jnp.mod(stop_num, cycle_stops), 1, keepdims=False
        )
        term = lax.dot_general(
            scaled, cov_slab, (((1,), (1,)), ((), ())), preferred_element_type=jnp.float32
        )
        return running + term

    initial = jnp.zeros((n_loads, row_count), jnp.float32)
    running = contribute(initial, start_block, base_stop)

    def onward(stop_num, carry):
        partial_sum, moving = carry
        moving = passed_along((moving[0], moving[1]), "blk", team_size)
        return (contribute(partial_sum, moving, base_stop - stop_num), moving)

    running, _ = lax.fori_loop(1, cycle_stops, onward, (running, start_block))
    product = lax.psum(running, "team")
    return product


def solution(mesh):
    placed = (P(None, ("blk", "team")), P(None, ("blk", "team")), P("blk", None, "team", None))
    return jax.shard_map(
        per_device, mesh=mesh, in_specs=placed, out_specs=P(None, "blk"), check_vma=False
    )
```

profile of v0, /device:TPU:1, one launch (start us, length us, event | category | flops | bytes accessed | tf_op | source)
XLA Modules:
  0.0 371.3 jit_solution(5446585981449639470)
XLA Ops:
  6.5 10.4 %all_gather.6 = bf16[64,1536]{1,0:T(8,128)(2,1)S(1)} all-gather(bf16[64,384]{1,0:T(8,128)(2,1)} %param.5), channel_id=1, replica_groups=mesh['blk'=64,'team'=4] {'team'}, dimensions={1}, use_global_device_ids=true | all-gather | bytes 245760 | tf_op jit(solution)/shard_map/all_gather | solution.py:21
  19.8 7.4 %all-gather = bf16[4,3,64]{2,1,0:T(4,128)(2,1)S(1)} all-gather(bf16[1,3,64]{2,1,0:T(4,128)(2,1)} %bitcast.55), channel_id=1, replica_groups=mesh['blk'=64,'team'=4] {'team'}, dimensions={0}, use_global_device_ids=true | all-gather | bytes 1920 | tf_op jit(solution)/shard_map/all_gather | solution.py:22
  31.2 6.3 %collective-permute-done.5 = bf16[64,12]{0,1:T(8,128)(2,1)S(1)} collective-permute-done((bf16[64,12]{0,1:T(8,128)(2,1)S(1)}, bf16[64,12]{0,1:T(8,128)(2,1)S(1)}, u32[]{:S(2)}, u32[]{:S(2)}) %collective-permute-start.5) | collective-permute-done | bytes 1568 | tf_op jit(solution)/shard_map/ppermute | solution.py:9
  42.7 13.0 %copy.27 = bf16[256,16,1,1536]{3,0,1,2:T(8,128)(2,1)} copy(bf16[256,16,1,1536]{3,1,2,0:T(8,128)(2,1)} %param.7) | data formatting | bytes 25165824 | tf_op args[2]
  56.8 219.6 %while.19 = (s32[]{:T(128)}, f32[64,256]{1,0:T(8,128)S(1)}, bf16[64,1536]{1,0:T(8,128)(2,1)S(1)}, bf16[64,12]{1,0:T(8,128)(2,1)S(1)}, s32[]{:T(128)}, /*index=5*...) while((s32[]{:T(128)}, f32[64,256]{1,0:T(8,128)S(1)}, ...), condition=%wide.region_1.2_spmd, body=%wide.region_0.1_spmd.sunk | while | flops 50642960 | bytes 3091284 | solution.py:65
  63.2 8.5 %collective-permute-done = bf16[64,12]{1,0:T(8,128)(2,1)S(1)} collective-permute-done((bf16[64,12]{1,0:T(8,128)(2,1)S(1)}, bf16[64,12]{1,0:T(8,128)(2,1)S(1)}, u32[]{:S(2)}, u32[]{:S(2)}) %collective-permute-start) | collective-permute-done | bytes 1568 | tf_op jit(solution)/shard_map/while/body/eval_jaxpr/ppermute | solution.py:9
  74.2 5.7 %collective-permute-start = (bf16[64,12]{1,0:T(8,128)(2,1)S(1)}, bf16[64,12]{1,0:T(8,128)(2,1)S(1)}, u32[]{:S(2)}, u32[]{:S(2)}) collective-permute-start(bf16[64,12]{1,0:T(8,128)(2,1)S(1)} %get-tuple-element.235), channel_id=1, source_target_pairs={{0,16},{4,20},{8,24},{12,28},{16,32},{20,36},{24,40},{28,44},{32,4... | collective-permute-start | bytes 4616 | tf_op jit(solution)/shard_map/while/body/eval_jaxpr/ppermute | solution.py:9
  79.9 11.1 %collective-permute-done = bf16[64,12]{1,0:T(8,128)(2,1)S(1)} collective-permute-done((bf16[64,12]{1,0:T(8,128)(2,1)S(1)}, bf16[64,12]{1,0:T(8,128)(2,1)S(1)}, u32[]{:S(2)}, u32[]{:S(2)}) %collective-permute-start) | collective-permute-done | bytes 1568 | tf_op jit(solution)/shard_map/while/body/eval_jaxpr/ppermute | solution.py:9
  94.8 10.4 %collective-permute-done = bf16[64,12]{1,0:T(8,128)(2,1)S(1)} collective-permute-done((bf16[64,12]{1,0:T(8,128)(2,1)S(1)}, bf16[64,12]{1,0:T(8,128)(2,1)S(1)}, u32[]{:S(2)}, u32[]{:S(2)}) %collective-permute-start) | collective-permute-done | bytes 1568 | tf_op jit(solution)/shard_map/while/body/eval_jaxpr/ppermute | solution.py:9
  110.6 8.2 %collective-permute-done = bf16[64,12]{1,0:T(8,128)(2,1)S(1)} collective-permute-done((bf16[64,12]{1,0:T(8,128)(2,1)S(1)}, bf16[64,12]{1,0:T(8,128)(2,1)S(1)}, u32[]{:S(2)}, u32[]{:S(2)}) %collective-permute-start) | collective-permute-done | bytes 1568 | tf_op jit(solution)/shard_map/while/body/eval_jaxpr/ppermute | solution.py:9
  125.2 7.1 %collective-permute-done = bf16[64,12]{1,0:T(8,128)(2,1)S(1)} collective-permute-done((bf16[64,12]{1,0:T(8,128)(2,1)S(1)}, bf16[64,12]{1,0:T(8,128)(2,1)S(1)}, u32[]{:S(2)}, u32[]{:S(2)}) %collective-permute-start) | collective-permute-done | bytes 1568 | tf_op jit(solution)/shard_map/while/body/eval_jaxpr/ppermute | solution.py:9
  134.1 5.4 %collective-permute-start = (bf16[64,12]{1,0:T(8,128)(2,1)S(1)}, bf16[64,12]{1,0:T(8,128)(2,1)S(1)}, u32[]{:S(2)}, u32[]{:S(2)}) collective-permute-start(bf16[64,12]{1,0:T(8,128)(2,1)S(1)} %get-tuple-element.235), channel_id=1, source_target_pairs={{0,16},{4,20},{8,24},{12,28},{16,32},{20,36},{24,40},{28,44},{32,4... | collective-permute-start | bytes 4616 | tf_op jit(solution)/shard_map/while/body/eval_jaxpr/ppermute | solution.py:9
  139.5 6.3 %collective-permute-done = bf16[64,12]{1,0:T(8,128)(2,1)S(1)} collective-permute-done((bf16[64,12]{1,0:T(8,128)(2,1)S(1)}, bf16[64,12]{1,0:T(8,128)(2,1)S(1)}, u32[]{:S(2)}, u32[]{:S(2)}) %collective-permute-start) | collective-permute-done | bytes 1568 | tf_op jit(solution)/shard_map/while/body/eval_jaxpr/ppermute | solution.py:9
  147.8 6.4 %collective-permute-start = (bf16[64,12]{1,0:T(8,128)(2,1)S(1)}, bf16[64,12]{1,0:T(8,128)(2,1)S(1)}, u32[]{:S(2)}, u32[]{:S(2)}) collective-permute-start(bf16[64,12]{1,0:T(8,128)(2,1)S(1)} %get-tuple-element.235), channel_id=1, source_target_pairs={{0,16},{4,20},{8,24},{12,28},{16,32},{20,36},{24,40},{28,44},{32,4... | collective-permute-start | bytes 4616 | tf_op jit(solution)/shard_map/while/body/eval_jaxpr/ppermute | solution.py:9
  154.2 5.0 %collective-permute-done = bf16[64,12]{1,0:T(8,128)(2,1)S(1)} collective-permute-done((bf16[64,12]{1,0:T(8,128)(2,1)S(1)}, bf16[64,12]{1,0:T(8,128)(2,1)S(1)}, u32[]{:S(2)}, u32[]{:S(2)}) %collective-permute-start) | collective-permute-done | bytes 1568 | tf_op jit(solution)/shard_map/while/body/eval_jaxpr/ppermute | solution.py:9
  165.6 7.0 %collective-permute-done = bf16[64,12]{1,0:T(8,128)(2,1)S(1)} collective-permute-done((bf16[64,12]{1,0:T(8,128)(2,1)S(1)}, bf16[64,12]{1,0:T(8,128)(2,1)S(1)}, u32[]{:S(2)}, u32[]{:S(2)}) %collective-permute-start) | collective-permute-done | bytes 1568 | tf_op jit(solution)/shard_map/while/body/eval_jaxpr/ppermute | solution.py:9
  177.0 10.0 %collective-permute-done = bf16[64,12]{1,0:T(8,128)(2,1)S(1)} collective-permute-done((bf16[64,12]{1,0:T(8,128)(2,1)S(1)}, bf16[64,12]{1,0:T(8,128)(2,1)S(1)}, u32[]{:S(2)}, u32[]{:S(2)}) %collective-permute-start) | collective-permute-done | bytes 1568 | tf_op jit(solution)/shard_map/while/body/eval_jaxpr/ppermute | solution.py:9
  190.2 12.2 %collective-permute-done = bf16[64,12]{1,0:T(8,128)(2,1)S(1)} collective-permute-done((bf16[64,12]{1,0:T(8,128)(2,1)S(1)}, bf16[64,12]{1,0:T(8,128)(2,1)S(1)}, u32[]{:S(2)}, u32[]{:S(2)}) %collective-permute-start) | collective-permute-done | bytes 1568 | tf_op jit(solution)/shard_map/while/body/eval_jaxpr/ppermute | solution.py:9
  204.3 13.2 %collective-permute-done = bf16[64,12]{1,0:T(8,128)(2,1)S(1)} collective-permute-done((bf16[64,12]{1,0:T(8,128)(2,1)S(1)}, bf16[64,12]{1,0:T(8,128)(2,1)S(1)}, u32[]{:S(2)}, u32[]{:S(2)}) %collective-permute-start) | collective-permute-done | bytes 1568 | tf_op jit(solution)/shard_map/while/body/eval_jaxpr/ppermute | solution.py:9
  219.4 14.1 %collective-permute-done = bf16[64,12]{1,0:T(8,128)(2,1)S(1)} collective-permute-done((bf16[64,12]{1,0:T(8,128)(2,1)S(1)}, bf16[64,12]{1,0:T(8,128)(2,1)S(1)}, u32[]{:S(2)}, u32[]{:S(2)}) %collective-permute-start) | collective-permute-done | bytes 1568 | tf_op jit(solution)/shard_map/while/body/eval_jaxpr/ppermute | solution.py:9
  235.5 12.3 %collective-permute-done = bf16[64,12]{1,0:T(8,128)(2,1)S(1)} collective-permute-done((bf16[64,12]{1,0:T(8,128)(2,1)S(1)}, bf16[64,12]{1,0:T(8,128)(2,1)S(1)}, u32[]{:S(2)}, u32[]{:S(2)}) %collective-permute-start) | collective-permute-done | bytes 1568 | tf_op jit(solution)/shard_map/while/body/eval_jaxpr/ppermute | solution.py:9
  250.1 11.1 %collective-permute-done = bf16[64,12]{1,0:T(8,128)(2,1)S(1)} collective-permute-done((bf16[64,12]{1,0:T(8,128)(2,1)S(1)}, bf16[64,12]{1,0:T(8,128)(2,1)S(1)}, u32[]{:S(2)}, u32[]{:S(2)}) %collective-permute-start) | collective-permute-done | bytes 1568 | tf_op jit(solution)/shard_map/while/body/eval_jaxpr/ppermute | solution.py:9
  264.2 10.6 %collective-permute-done = bf16[64,12]{1,0:T(8,128)(2,1)S(1)} collective-permute-done((bf16[64,12]{1,0:T(8,128)(2,1)S(1)}, bf16[64,12]{1,0:T(8,128)(2,1)S(1)}, u32[]{:S(2)}, u32[]{:S(2)}) %collective-permute-start) | collective-permute-done | bytes 1568 | tf_op jit(solution)/shard_map/while/body/eval_jaxpr/ppermute | solution.py:9
  277.1 85.8 %all-reduce.2.cloned.1.call-done = f32[64,256]{1,0:T(8,128)} async-done(((f32[64,256]{1,0:T(8,128)}), f32[64,256]{1,0:T(8,128)}) %all-reduce.2.cloned.1.call-update) | async-done | bytes 65552 | tf_op jit(solution)/shard_map/psum | solution.py:66
  (127 shorter events, 69.8 us)
Async XLA Ops:
  6.5 356.4 %all-reduce.2.cloned.1.call-start = ((), (), s32[]{:S(2)}) async-start(), calls=%async_computation | async-start | bytes 131072 | tf_op jit(solution)/shard_map/psum | solution.py:66
  16.9 20.6 %collective-permute-start.2 = (bf16[64,1536]{1,0:T(8,128)(2,1)S(1)}, bf16[64,1536]{1,0:T(8,128)(2,1)S(1)}, u32[]{:S(2)}, u32[]{:S(2)}) collective-permute-start(bf16[64,1536]{1,0:T(8,128)(2,1)S(1)} %all_gather.6), channel_id=1, source_target_pairs={{0,4},{4,8},{8,12},{12,16},{16,20},{20,24},{24,28},{28,32},{32,36}... | collective-permute-start | bytes 589832 | tf_op jit(solution)/shard_map/ppermute | solution.py:9
  16.9 39.0 %collective-permute-start.3 = (bf16[64,1536]{1,0:T(8,128)(2,1)S(1)}, bf16[64,1536]{1,0:T(8,128)(2,1)S(1)}, u32[]{:S(2)}, u32[]{:S(2)}) collective-permute-start(bf16[64,1536]{1,0:T(8,128)(2,1)S(1)} %all_gather.6), channel_id=1, source_target_pairs={{0,8},{4,12},{8,16},{12,20},{16,24},{20,28},{24,32},{28,36},{32,40... | collective-permute-start | bytes 589832 | tf_op jit(solution)/shard_map/ppermute | solution.py:9
  30.0 25.6 %collective-permute-start.6 = (bf16[64,12]{0,1:T(8,128)(2,1)S(1)}, bf16[64,12]{0,1:T(8,128)(2,1)S(1)}, u32[]{:S(2)}, u32[]{:S(2)}) collective-permute-start(bf16[64,12]{0,1:T(8,128)(2,1)S(1)} %bitcast.50), channel_id=1, source_target_pairs={{0,8},{4,12},{8,16},{12,20},{16,24},{20,28},{24,32},{28,36},{32,40... | collective-permute-start | bytes 4616 | tf_op jit(solution)/shard_map/ppermute | solution.py:9
  37.6 18.1 %collective-permute-start.7 = (bf16[64,12]{0,1:T(8,128)(2,1)S(1)}, bf16[64,12]{0,1:T(8,128)(2,1)S(1)}, u32[]{:S(2)}, u32[]{:S(2)}) collective-permute-start(bf16[64,12]{0,1:T(8,128)(2,1)S(1)} %collective-permute-done.5), channel_id=1, source_target_pairs={{0,8},{4,12},{8,16},{12,20},{16,24},{20,28},{24,32},{28,36},{32,40... | collective-permute-start | bytes 4616 | tf_op jit(solution)/shard_map/ppermute | solution.py:9
  37.6 18.4 %collective-permute-start.4 = (bf16[64,1536]{1,0:T(8,128)(2,1)S(1)}, bf16[64,1536]{1,0:T(8,128)(2,1)S(1)}, u32[]{:S(2)}, u32[]{:S(2)}) collective-permute-start(bf16[64,1536]{1,0:T(8,128)(2,1)S(1)} %collective-permute-done.2), channel_id=1, source_target_pairs={{0,8},{4,12},{8,16},{12,20},{16,24},{20,28},{24,32},{28,36},{32,40... | collective-permute-start | bytes 589832 | tf_op jit(solution)/shard_map/ppermute | solution.py:9
  56.9 14.9 %collective-permute-start.1 = (bf16[64,1536]{1,0:T(8,128)(2,1)S(1)}, bf16[64,1536]{1,0:T(8,128)(2,1)S(1)}, u32[]{:S(2)}, u32[]{:S(2)}) collective-permute-start(bf16[64,1536]{1,0:T(8,128)(2,1)S(1)} %get-tuple-element.234), channel_id=1, source_target_pairs={{0,16},{4,20},{8,24},{12,28},{16,32},{20,36},{24,40},{28,44},{32,4... | collective-permute-start | bytes 589832 | tf_op jit(solution)/shard_map/while/body/eval_jaxpr/ppermute | solution.py:9
  59.4 12.3 %collective-permute-start = (bf16[64,12]{1,0:T(8,128)(2,1)S(1)}, bf16[64,12]{1,0:T(8,128)(2,1)S(1)}, u32[]{:S(2)}, u32[]{:S(2)}) collective-permute-start(bf16[64,12]{1,0:T(8,128)(2,1)S(1)} %get-tuple-element.235), channel_id=1, source_target_pairs={{0,16},{4,20},{8,24},{12,28},{16,32},{20,36},{24,40},{28,44},{32,4... | collective-permute-start | bytes 4616 | tf_op jit(solution)/shard_map/while/body/eval_jaxpr/ppermute | solution.py:9
  73.4 17.6 %collective-permute-start.1 = (bf16[64,1536]{1,0:T(8,128)(2,1)S(1)}, bf16[64,1536]{1,0:T(8,128)(2,1)S(1)}, u32[]{:S(2)}, u32[]{:S(2)}) collective-permute-start(bf16[64,1536]{1,0:T(8,128)(2,1)S(1)} %get-tuple-element.234), channel_id=1, source_target_pairs={{0,16},{4,20},{8,24},{12,28},{16,32},{20,36},{24,40},{28,44},{32,4... | collective-permute-start | bytes 589832 | tf_op jit(solution)/shard_map/while/body/eval_jaxpr/ppermute | solution.py:9
  74.2 16.8 %collective-permute-start = (bf16[64,12]{1,0:T(8,128)(2,1)S(1)}, bf16[64,12]{1,0:T(8,128)(2,1)S(1)}, u32[]{:S(2)}, u32[]{:S(2)}) collective-permute-start(bf16[64,12]{1,0:T(8,128)(2,1)S(1)} %get-tuple-element.235), channel_id=1, source_target_pairs={{0,16},{4,20},{8,24},{12,28},{16,32},{20,36},{24,40},{28,44},{32,4... | collective-permute-start | bytes 4616 | tf_op jit(solution)/shard_map/while/body/eval_jaxpr/ppermute | solution.py:9
  92.7 12.5 %collective-permute-start.1 = (bf16[64,1536]{1,0:T(8,128)(2,1)S(1)}, bf16[64,1536]{1,0:T(8,128)(2,1)S(1)}, u32[]{:S(2)}, u32[]{:S(2)}) collective-permute-start(bf16[64,1536]{1,0:T(8,128)(2,1)S(1)} %get-tuple-element.234), channel_id=1, source_target_pairs={{0,16},{4,20},{8,24},{12,28},{16,32},{20,36},{24,40},{28,44},{32,4... | collective-permute-start | bytes 589832 | tf_op jit(solution)/shard_map/while/body/eval_jaxpr/ppermute | solution.py:9
  92.8 12.4 %collective-permute-start = (bf16[64,12]{1,0:T(8,128)(2,1)S(1)}, bf16[64,12]{1,0:T(8,128)(2,1)S(1)}, u32[]{:S(2)}, u32[]{:S(2)}) collective-permute-start(bf16[64,12]{1,0:T(8,128)(2,1)S(1)} %get-tuple-element.235), channel_id=1, source_target_pairs={{0,16},{4,20},{8,24},{12,28},{16,32},{20,36},{24,40},{28,44},{32,4... | collective-permute-start | bytes 4616 | tf_op jit(solution)/shard_map/while/body/eval_jaxpr/ppermute | solution.py:9
  106.9 11.9 %collective-permute-start.1 = (bf16[64,1536]{1,0:T(8,128)(2,1)S(1)}, bf16[64,1536]{1,0:T(8,128)(2,1)S(1)}, u32[]{:S(2)}, u32[]{:S(2)}) collective-permute-start(bf16[64,1536]{1,0:T(8,128)(2,1)S(1)} %get-tuple-element.234), channel_id=1, source_target_pairs={{0,16},{4,20},{8,24},{12,28},{16,32},{20,36},{24,40},{28,44},{32,4... | collective-permute-start | bytes 589832 | tf_op jit(solution)/shard_map/while/body/eval_jaxpr/ppermute | solution.py:9
  120.5 11.8 %collective-permute-start.1 = (bf16[64,1536]{1,0:T(8,128)(2,1)S(1)}, bf16[64,1536]{1,0:T(8,128)(2,1)S(1)}, u32[]{:S(2)}, u32[]{:S(2)}) collective-permute-start(bf16[64,1536]{1,0:T(8,128)(2,1)S(1)} %get-tuple-element.234), channel_id=1, source_target_pairs={{0,16},{4,20},{8,24},{12,28},{16,32},{20,36},{24,40},{28,44},{32,4... | collective-permute-start | bytes 589832 | tf_op jit(solution)/shard_map/while/body/eval_jaxpr/ppermute | solution.py:9
  174.3 12.6 %collective-permute-start.1 = (bf16[64,1536]{1,0:T(8,128)(2,1)S(1)}, bf16[64,1536]{1,0:T(8,128)(2,1)S(1)}, u32[]{:S(2)}, u32[]{:S(2)}) collective-permute-start(bf16[64,1536]{1,0:T(8,128)(2,1)S(1)} %get-tuple-element.234), channel_id=1, source_target_pairs={{0,16},{4,20},{8,24},{12,28},{16,32},{20,36},{24,40},{28,44},{32,4... | collective-permute-start | bytes 589832 | tf_op jit(solution)/shard_map/while/body/eval_jaxpr/ppermute | solution.py:9
  175.1 11.8 %collective-permute-start = (bf16[64,12]{1,0:T(8,128)(2,1)S(1)}, bf16[64,12]{1,0:T(8,128)(2,1)S(1)}, u32[]{:S(2)}, u32[]{:S(2)}) collective-permute-start(bf16[64,12]{1,0:T(8,128)(2,1)S(1)} %get-tuple-element.235), channel_id=1, source_target_pairs={{0,16},{4,20},{8,24},{12,28},{16,32},{20,36},{24,40},{28,44},{32,4... | collective-permute-start | bytes 4616 | tf_op jit(solution)/shard_map/while/body/eval_jaxpr/ppermute | solution.py:9
  188.6 13.7 %collective-permute-start.1 = (bf16[64,1536]{1,0:T(8,128)(2,1)S(1)}, bf16[64,1536]{1,0:T(8,128)(2,1)S(1)}, u32[]{:S(2)}, u32[]{:S(2)}) collective-permute-start(bf16[64,1536]{1,0:T(8,128)(2,1)S(1)} %get-tuple-element.234), channel_id=1, source_target_pairs={{0,16},{4,20},{8,24},{12,28},{16,32},{20,36},{24,40},{28,44},{32,4... | collective-permute-start | bytes 589832 | tf_op jit(solution)/shard_map/while/body/eval_jaxpr/ppermute | solution.py:9
  188.7 13.6 %collective-permute-start = (bf16[64,12]{1,0:T(8,128)(2,1)S(1)}, bf16[64,12]{1,0:T(8,128)(2,1)S(1)}, u32[]{:S(2)}, u32[]{:S(2)}) collective-permute-start(bf16[64,12]{1,0:T(8,128)(2,1)S(1)} %get-tuple-element.235), channel_id=1, source_target_pairs={{0,16},{4,20},{8,24},{12,28},{16,32},{20,36},{24,40},{28,44},{32,4... | collective-permute-start | bytes 4616 | tf_op jit(solution)/shard_map/while/body/eval_jaxpr/ppermute | solution.py:9
  204.1 13.4 %collective-permute-start.1 = (bf16[64,1536]{1,0:T(8,128)(2,1)S(1)}, bf16[64,1536]{1,0:T(8,128)(2,1)S(1)}, u32[]{:S(2)}, u32[]{:S(2)}) collective-permute-start(bf16[64,1536]{1,0:T(8,128)(2,1)S(1)} %get-tuple-element.234), channel_id=1, source_target_pairs={{0,16},{4,20},{8,24},{12,28},{16,32},{20,36},{24,40},{28,44},{32,4... | collective-permute-start | bytes 589832 | tf_op jit(solution)/shard_map/while/body/eval_jaxpr/ppermute | solution.py:9
  204.1 13.3 %collective-permute-start = (bf16[64,12]{1,0:T(8,128)(2,1)S(1)}, bf16[64,12]{1,0:T(8,128)(2,1)S(1)}, u32[]{:S(2)}, u32[]{:S(2)}) collective-permute-start(bf16[64,12]{1,0:T(8,128)(2,1)S(1)} %get-tuple-element.235), channel_id=1, source_target_pairs={{0,16},{4,20},{8,24},{12,28},{16,32},{20,36},{24,40},{28,44},{32,4... | collective-permute-start | bytes 4616 | tf_op jit(solution)/shard_map/while/body/eval_jaxpr/ppermute | solution.py:9
  219.2 14.4 %collective-permute-start.1 = (bf16[64,1536]{1,0:T(8,128)(2,1)S(1)}, bf16[64,1536]{1,0:T(8,128)(2,1)S(1)}, u32[]{:S(2)}, u32[]{:S(2)}) collective-permute-start(bf16[64,1536]{1,0:T(8,128)(2,1)S(1)} %get-tuple-element.234), channel_id=1, source_target_pairs={{0,16},{4,20},{8,24},{12,28},{16,32},{20,36},{24,40},{28,44},{32,4... | collective-permute-start | bytes 589832 | tf_op jit(solution)/shard_map/while/body/eval_jaxpr/ppermute | solution.py:9
  219.3 14.3 %collective-permute-start = (bf16[64,12]{1,0:T(8,128)(2,1)S(1)}, bf16[64,12]{1,0:T(8,128)(2,1)S(1)}, u32[]{:S(2)}, u32[]{:S(2)}) collective-permute-start(bf16[64,12]{1,0:T(8,128)(2,1)S(1)} %get-tuple-element.235), channel_id=1, source_target_pairs={{0,16},{4,20},{8,24},{12,28},{16,32},{20,36},{24,40},{28,44},{32,4... | collective-permute-start | bytes 4616 | tf_op jit(solution)/shard_map/while/body/eval_jaxpr/ppermute | solution.py:9
  235.3 12.5 %collective-permute-start.1 = (bf16[64,1536]{1,0:T(8,128)(2,1)S(1)}, bf16[64,1536]{1,0:T(8,128)(2,1)S(1)}, u32[]{:S(2)}, u32[]{:S(2)}) collective-permute-start(bf16[64,1536]{1,0:T(8,128)(2,1)S(1)} %get-tuple-element.234), channel_id=1, source_target_pairs={{0,16},{4,20},{8,24},{12,28},{16,32},{20,36},{24,40},{28,44},{32,4... | collective-permute-start | bytes 589832 | tf_op jit(solution)/shard_map/while/body/eval_jaxpr/ppermute | solution.py:9
  235.4 12.4 %collective-permute-start = (bf16[64,12]{1,0:T(8,128)(2,1)S(1)}, bf16[64,12]{1,0:T(8,128)(2,1)S(1)}, u32[]{:S(2)}, u32[]{:S(2)}) collective-permute-start(bf16[64,12]{1,0:T(8,128)(2,1)S(1)} %get-tuple-element.235), channel_id=1, source_target_pairs={{0,16},{4,20},{8,24},{12,28},{16,32},{20,36},{24,40},{28,44},{32,4... | collective-permute-start | bytes 4616 | tf_op jit(solution)/shard_map/while/body/eval_jaxpr/ppermute | solution.py:9
  (14 other events, 149.6 us)
Sparse Core Ops, SparseCore 0:
  277.2 85.6 all-reduce.1
where the time goes:
time: 372 us; the launch traced here: 371 us
  waiting for transfers between devices  239 us (64%)
  starting transfers between devices  54.3 us (15%)
  local copies, waits for them, and re-layouts  23 us (6%)
  matrix products  22.6 us (6%)
  blocking collectives  17.7 us (5%)
  between operations  13.5 us (4%)
    ppermute x36, waiting for transfers between devices, passed_along(): return lax.ppermute(x, axis, [(i, (i + by) % size) for i in range(size)])  153 us
    psum x1, waiting for transfers between devices, per_device(): product = lax.psum(running, 'team')  85.8 us
    ppermute x36, starting transfers between devices, passed_along(): return lax.ppermute(x, axis, [(i, (i + by) % size) for i in range(size)])  54.3 us
    dot_general x16, matrix products, contribute(): lax.dot_general(scaled, cov_slab, (((1,), (1,)), ((), ())), preferred_ele...  22.6 us
    unnamed x5, local copies, waits for them, and re-layouts  15.1 us
    all_gather x1, blocking collectives, per_device(): lax.all_gather(loadings, 'team', axis=1, tiled=True)  10.4 us
  transfers between devices with their start and end apart: 37, of which 17 were waited for; matrix products, arithmetic and copies ran while one was open for 5% of the time, Pallas kernels for 0%

commit v1 on v0

--- a/solution.py
+++ b/solution.py
@@ -18,7 +18,9 @@
     skew_lag = jnp.mod(cycle_pos - member, team_size)
     base_stop = jnp.mod((cycle_pos - skew_lag - member) // team_size, cycle_stops)
     held_block = (
-        lax.all_gather(loadings, "team", axis=1, tiled=True),
+        jnp.concatenate(
+            lax.all_to_all(jnp.stack([loadings] * lax.axis_size("team")), "team", 0, 0), axis=1
+        ),
         lax.all_gather(scales, "team", axis=1, tiled=True),
     )
     near_copy = passed_along((held_block[0], held_block[1]), "blk", 1)

time: 372 us -> 366 us (0.984)
  starting transfers between devices: 54.3 us -> 42.3 us
    ppermute x36, waiting for transfers between devices: 153 us -> 179 us  [passed_along(): return lax.ppermute(x, axis, [(i, (i + by) % size) for i in range(size)])]
    psum x1, waiting for transfers between devices: 85.8 us -> 63.2 us  [per_device(): product = lax.psum(running, 'team')]
    ppermute x36, starting transfers between devices: 54.3 us -> 42.3 us  [passed_along(): return lax.ppermute(x, axis, [(i, (i + by) % size) for i in range(size)])]
    all_to_all x0 -> x1, blocking collectives: none -> 11.7 us  [per_device(): lax.all_to_all(jnp.stack([loadings] * lax.axis_size('team')), 'team', 0, 0)]
    all_gather x1 -> x0, blocking collectives: 10.4 us -> none  [per_device(): lax.all_gather(loadings, 'team', axis=1, tiled=True)]
  transfers between devices with their start and end apart: 37 -> 37, of which waited for: 17 -> 18; matrix products, arithmetic and copies ran while one was open for 5% -> 5% of each run, Pallas kernels for 0% -> 0%
where the time goes in v1:
time: 366 us; the launch traced here: 365 us
  waiting for transfers between devices  242 us (66%)
  starting transfers between devices  42.3 us (12%)
  local copies, waits for them, and re-layouts  24 us (7%)
  matrix products  22.5 us (6%)
  blocking collectives  19.4 us (5%)
  between operations  13.5 us (4%)
    ppermute x36, waiting for transfers between devices, passed_along(): return lax.ppermute(x, axis, [(i, (i + by) % size) for i in range(size)])  179 us
    psum x1, waiting for transfers between devices, per_device(): product = lax.psum(running, 'team')  63.2 us
    ppermute x36, starting transfers between devices, passed_along(): return lax.ppermute(x, axis, [(i, (i + by) % size) for i in range(size)])  42.3 us
    dot_general x16, matrix products, contribute(): lax.dot_general(scaled, cov_slab, (((1,), (1,)), ((), ())), preferred_ele...  22.5 us
    unnamed x5, local copies, waits for them, and re-layouts  15.1 us
    all_to_all x1, blocking collectives, per_device(): lax.all_to_all(jnp.stack([loadings] * lax.axis_size('team')), 'team', 0, 0)  11.7 us
    all_gather x1, blocking collectives, per_device(): lax.all_gather(scales, 'team', axis=1, tiled=True)  7.65 us
  transfers between devices with their start and end apart: 37, of which 18 were waited for; matrix products, arithmetic and copies ran while one was open for 5% of the time, Pallas kernels for 0%

profile of v1, /device:TPU:1, one launch (start us, length us, event | category | flops | bytes accessed | tf_op | source)
XLA Modules:
  0.0 365.0 jit_solution(18233982713644026447)
XLA Ops:
  7.4 11.7 %all_to_all.5 = bf16[4,64,384]{2,1,0:T(8,128)(2,1)S(1)} all-to-all(bf16[4,64,384]{2,1,0:T(8,128)(2,1)S(1)} %stack.34), channel_id=1, replica_groups=mesh['blk'=64,'team'=4] {'team'}, dimensions={0} | all-to-all | bytes 393216 | tf_op jit(solution)/shard_map/all_to_all | solution.py:22
  20.8 7.7 %all-gather = bf16[4,3,64]{2,1,0:T(4,128)(2,1)S(1)} all-gather(bf16[1,3,64]{2,1,0:T(4,128)(2,1)} %bitcast.60), channel_id=1, replica_groups=mesh['blk'=64,'team'=4] {'team'}, dimensions={0}, use_global_device_ids=true | all-gather | bytes 1920 | tf_op jit(solution)/shard_map/all_gather | solution.py:24
  30.1 4.2 %collective-permute-start.6 = (bf16[64,12]{0,1:T(8,128)(2,1)S(1)}, bf16[64,12]{0,1:T(8,128)(2,1)S(1)}, u32[]{:S(2)}, u32[]{:S(2)}) collective-permute-start(bf16[64,12]{0,1:T(8,128)(2,1)S(1)} %bitcast.55), channel_id=1, source_target_pairs={{0,8},{4,12},{8,16},{12,20},{16,24},{20,28},{24,32},{28,36},{32,40... | collective-permute-start | bytes 4616 | tf_op jit(solution)/shard_map/ppermute | solution.py:9
  38.5 4.4 %constant_dynamic-slice_fusion = bf16[256,1,1,1536]{3,1,2,0:T(2,128)(2,1)S(1)} fusion(bf16[256,16,1,1536]{3,1,2,0:T(8,128)(2,1)} %param.7, s32[]{:T(128)S(6)} %select_n.61), kind=kLoop, calls=%fused_computation.27 | loop fusion | bytes 1572868 | tf_op jit(solution)/shard_map/jit(dynamic_index_in_dim)/dynamic_slice | solution.py:51
  42.9 13.0 %copy.34 = bf16[256,16,1,1536]{3,0,1,2:T(8,128)(2,1)} copy(bf16[256,16,1,1536]{3,1,2,0:T(8,128)(2,1)} %param.7) | data formatting | bytes 25165824 | tf_op args[2]
  60.8 232.1 %while.19 = (s32[]{:T(128)}, f32[64,256]{1,0:T(8,128)S(1)}, bf16[64,1536]{1,0:T(8,128)(2,1)S(1)}, bf16[64,12]{1,0:T(8,128)(2,1)S(1)}, s32[]{:T(128)}, /*index=5*...) while((s32[]{:T(128)}, f32[64,256]{1,0:T(8,128)S(1)}, ...), condition=%wide.region_1.2_spmd, body=%wide.region_0.1_spmd.sunk | while | flops 50642960 | bytes 3091284 | solution.py:67
  63.6 14.7 %collective-permute-done = bf16[64,12]{1,0:T(8,128)(2,1)S(1)} collective-permute-done((bf16[64,12]{1,0:T(8,128)(2,1)S(1)}, bf16[64,12]{1,0:T(8,128)(2,1)S(1)}, u32[]{:S(2)}, u32[]{:S(2)}) %collective-permute-start) | collective-permute-done | bytes 1568 | tf_op jit(solution)/shard_map/while/body/eval_jaxpr/ppermute | solution.py:9
  80.2 16.7 %collective-permute-done = bf16[64,12]{1,0:T(8,128)(2,1)S(1)} collective-permute-done((bf16[64,12]{1,0:T(8,128)(2,1)S(1)}, bf16[64,12]{1,0:T(8,128)(2,1)S(1)}, u32[]{:S(2)}, u32[]{:S(2)}) %collective-permute-start) | collective-permute-done | bytes 1568 | tf_op jit(solution)/shard_map/while/body/eval_jaxpr/ppermute | solution.py:9
  98.9 13.0 %collective-permute-done = bf16[64,12]{1,0:T(8,128)(2,1)S(1)} collective-permute-done((bf16[64,12]{1,0:T(8,128)(2,1)S(1)}, bf16[64,12]{1,0:T(8,128)(2,1)S(1)}, u32[]{:S(2)}, u32[]{:S(2)}) %collective-permute-start) | collective-permute-done | bytes 1568 | tf_op jit(solution)/shard_map/while/body/eval_jaxpr/ppermute | solution.py:9
  114.9 11.1 %collective-permute-done = bf16[64,12]{1,0:T(8,128)(2,1)S(1)} collective-permute-done((bf16[64,12]{1,0:T(8,128)(2,1)S(1)}, bf16[64,12]{1,0:T(8,128)(2,1)S(1)}, u32[]{:S(2)}, u32[]{:S(2)}) %collective-permute-start) | collective-permute-done | bytes 1568 | tf_op jit(solution)/shard_map/while/body/eval_jaxpr/ppermute | solution.py:9
  129.9 9.5 %collective-permute-done = bf16[64,12]{1,0:T(8,128)(2,1)S(1)} collective-permute-done((bf16[64,12]{1,0:T(8,128)(2,1)S(1)}, bf16[64,12]{1,0:T(8,128)(2,1)S(1)}, u32[]{:S(2)}, u32[]{:S(2)}) %collective-permute-start) | collective-permute-done | bytes 1568 | tf_op jit(solution)/shard_map/while/body/eval_jaxpr/ppermute | solution.py:9
  143.9 9.0 %collective-permute-done = bf16[64,12]{1,0:T(8,128)(2,1)S(1)} collective-permute-done((bf16[64,12]{1,0:T(8,128)(2,1)S(1)}, bf16[64,12]{1,0:T(8,128)(2,1)S(1)}, u32[]{:S(2)}, u32[]{:S(2)}) %collective-permute-start) | collective-permute-done | bytes 1568 | tf_op jit(solution)/shard_map/while/body/eval_jaxpr/ppermute | solution.py:9
  154.7 5.0 %collective-permute-start = (bf16[64,12]{1,0:T(8,128)(2,1)S(1)}, bf16[64,12]{1,0:T(8,128)(2,1)S(1)}, u32[]{:S(2)}, u32[]{:S(2)}) collective-permute-start(bf16[64,12]{1,0:T(8,128)(2,1)S(1)} %get-tuple-element.241), channel_id=1, source_target_pairs={{0,16},{4,20},{8,24},{12,28},{16,32},{20,36},{24,40},{28,44},{32,4... | collective-permute-start | bytes 4616 | tf_op jit(solution)/shard_map/while/body/eval_jaxpr/ppermute | solution.py:9
  159.7 6.6 %collective-permute-done = bf16[64,12]{1,0:T(8,128)(2,1)S(1)} collective-permute-done((bf16[64,12]{1,0:T(8,128)(2,1)S(1)}, bf16[64,12]{1,0:T(8,128)(2,1)S(1)}, u32[]{:S(2)}, u32[]{:S(2)}) %collective-permute-start) | collective-permute-done | bytes 1568 | tf_op jit(solution)/shard_map/while/body/eval_jaxpr/ppermute | solution.py:9
  168.5 6.1 %collective-permute-start = (bf16[64,12]{1,0:T(8,128)(2,1)S(1)}, bf16[64,12]{1,0:T(8,128)(2,1)S(1)}, u32[]{:S(2)}, u32[]{:S(2)}) collective-permute-start(bf16[64,12]{1,0:T(8,128)(2,1)S(1)} %get-tuple-element.241), channel_id=1, source_target_pairs={{0,16},{4,20},{8,24},{12,28},{16,32},{20,36},{24,40},{28,44},{32,4... | collective-permute-start | bytes 4616 | tf_op jit(solution)/shard_map/while/body/eval_jaxpr/ppermute | solution.py:9
  174.6 5.6 %collective-permute-done = bf16[64,12]{1,0:T(8,128)(2,1)S(1)} collective-permute-done((bf16[64,12]{1,0:T(8,128)(2,1)S(1)}, bf16[64,12]{1,0:T(8,128)(2,1)S(1)}, u32[]{:S(2)}, u32[]{:S(2)}) %collective-permute-start) | collective-permute-done | bytes 1568 | tf_op jit(solution)/shard_map/while/body/eval_jaxpr/ppermute | solution.py:9
  186.4 7.3 %collective-permute-done = bf16[64,12]{1,0:T(8,128)(2,1)S(1)} collective-permute-done((bf16[64,12]{1,0:T(8,128)(2,1)S(1)}, bf16[64,12]{1,0:T(8,128)(2,1)S(1)}, u32[]{:S(2)}, u32[]{:S(2)}) %collective-permute-start) | collective-permute-done | bytes 1568 | tf_op jit(solution)/shard_map/while/body/eval_jaxpr/ppermute | solution.py:9
  197.7 9.7 %collective-permute-done = bf16[64,12]{1,0:T(8,128)(2,1)S(1)} collective-permute-done((bf16[64,12]{1,0:T(8,128)(2,1)S(1)}, bf16[64,12]{1,0:T(8,128)(2,1)S(1)}, u32[]{:S(2)}, u32[]{:S(2)}) %collective-permute-start) | collective-permute-done | bytes 1568 | tf_op jit(solution)/shard_map/while/body/eval_jaxpr/ppermute | solution.py:9
  211.4 10.6 %collective-permute-done = bf16[64,12]{1,0:T(8,128)(2,1)S(1)} collective-permute-done((bf16[64,12]{1,0:T(8,128)(2,1)S(1)}, bf16[64,12]{1,0:T(8,128)(2,1)S(1)}, u32[]{:S(2)}, u32[]{:S(2)}) %collective-permute-start) | collective-permute-done | bytes 1568 | tf_op jit(solution)/shard_map/while/body/eval_jaxpr/ppermute | solution.py:9
  224.7 13.7 %collective-permute-done = bf16[64,12]{1,0:T(8,128)(2,1)S(1)} collective-permute-done((bf16[64,12]{1,0:T(8,128)(2,1)S(1)}, bf16[64,12]{1,0:T(8,128)(2,1)S(1)}, u32[]{:S(2)}, u32[]{:S(2)}) %collective-permute-start) | collective-permute-done | bytes 1568 | tf_op jit(solution)/shard_map/while/body/eval_jaxpr/ppermute | solution.py:9
  240.3 14.7 %collective-permute-done = bf16[64,12]{1,0:T(8,128)(2,1)S(1)} collective-permute-done((bf16[64,12]{1,0:T(8,128)(2,1)S(1)}, bf16[64,12]{1,0:T(8,128)(2,1)S(1)}, u32[]{:S(2)}, u32[]{:S(2)}) %collective-permute-start) | collective-permute-done | bytes 1568 | tf_op jit(solution)/shard_map/while/body/eval_jaxpr/ppermute | solution.py:9
  257.2 16.0 %collective-permute-done = bf16[64,12]{1,0:T(8,128)(2,1)S(1)} collective-permute-done((bf16[64,12]{1,0:T(8,128)(2,1)S(1)}, bf16[64,12]{1,0:T(8,128)(2,1)S(1)}, u32[]{:S(2)}, u32[]{:S(2)}) %collective-permute-start) | collective-permute-done | bytes 1568 | tf_op jit(solution)/shard_map/while/body/eval_jaxpr/ppermute | solution.py:9
  275.1 16.0 %collective-permute-done = bf16[64,12]{1,0:T(8,128)(2,1)S(1)} collective-permute-done((bf16[64,12]{1,0:T(8,128)(2,1)S(1)}, bf16[64,12]{1,0:T(8,128)(2,1)S(1)}, u32[]{:S(2)}, u32[]{:S(2)}) %collective-permute-start) | collective-permute-done | bytes 1568 | tf_op jit(solution)/shard_map/while/body/eval_jaxpr/ppermute | solution.py:9
  293.5 63.2 %all-reduce.2.cloned.1.call-done = f32[64,256]{1,0:T(8,128)} async-done(((f32[64,256]{1,0:T(8,128)}), f32[64,256]{1,0:T(8,128)}) %all-reduce.2.cloned.1.call-update) | async-done | bytes 65552 | tf_op jit(solution)/shard_map/psum | solution.py:68
  (131 shorter events, 61.3 us)
Async XLA Ops:
  6.5 350.2 %all-reduce.2.cloned.1.call-start = ((), (), s32[]{:S(2)}) async-start(), calls=%async_computation.1 | async-start | bytes 131072 | tf_op jit(solution)/shard_map/psum | solution.py:68
  19.1 19.4 %collective-permute-start.2 = (bf16[64,1536]{1,0:T(8,128)(2,1)S(1)}, bf16[64,1536]{1,0:T(8,128)(2,1)S(1)}, u32[]{:S(2)}, u32[]{:S(2)}) collective-permute-start(bf16[64,1536]{1,0:T(8,128)(2,1)S(1)} %bitcast.52), channel_id=1, source_target_pairs={{0,4},{4,8},{8,12},{12,16},{16,20},{20,24},{24,28},{28,32},{32,36}... | collective-permute-start | bytes 589832 | tf_op jit(solution)/shard_map/ppermute | solution.py:9
  30.1 25.8 %collective-permute-start.6 = (bf16[64,12]{0,1:T(8,128)(2,1)S(1)}, bf16[64,12]{0,1:T(8,128)(2,1)S(1)}, u32[]{:S(2)}, u32[]{:S(2)}) collective-permute-start(bf16[64,12]{0,1:T(8,128)(2,1)S(1)} %bitcast.55), channel_id=1, source_target_pairs={{0,8},{4,12},{8,16},{12,20},{16,24},{20,28},{24,32},{28,36},{32,40... | collective-permute-start | bytes 4616 | tf_op jit(solution)/shard_map/ppermute | solution.py:9
  35.6 20.3 %collective-permute-start.7 = (bf16[64,12]{0,1:T(8,128)(2,1)S(1)}, bf16[64,12]{0,1:T(8,128)(2,1)S(1)}, u32[]{:S(2)}, u32[]{:S(2)}) collective-permute-start(bf16[64,12]{0,1:T(8,128)(2,1)S(1)} %collective-permute-done.5), channel_id=1, source_target_pairs={{0,8},{4,12},{8,16},{12,20},{16,24},{20,28},{24,32},{28,36},{32,40... | collective-permute-start | bytes 4616 | tf_op jit(solution)/shard_map/ppermute | solution.py:9
  35.6 20.8 %collective-permute-start.3 = (bf16[64,1536]{1,0:T(8,128)(2,1)S(1)}, bf16[64,1536]{1,0:T(8,128)(2,1)S(1)}, u32[]{:S(2)}, u32[]{:S(2)}) collective-permute-start(bf16[64,1536]{1,0:T(8,128)(2,1)S(1)} %bitcast.53), channel_id=1, source_target_pairs={{0,8},{4,12},{8,16},{12,20},{16,24},{20,28},{24,32},{28,36},{32,40... | collective-permute-start | bytes 589832 | tf_op jit(solution)/shard_map/ppermute | solution.py:9
  38.4 21.5 %collective-permute-start.4 = (bf16[64,1536]{1,0:T(8,128)(2,1)S(1)}, bf16[64,1536]{1,0:T(8,128)(2,1)S(1)}, u32[]{:S(2)}, u32[]{:S(2)}) collective-permute-start(bf16[64,1536]{1,0:T(8,128)(2,1)S(1)} %collective-permute-done.2), channel_id=1, source_target_pairs={{0,8},{4,12},{8,16},{12,20},{16,24},{20,28},{24,32},{28,36},{32,40... | collective-permute-start | bytes 589832 | tf_op jit(solution)/shard_map/ppermute | solution.py:9
  60.8 17.5 %collective-permute-start.1 = (bf16[64,1536]{1,0:T(8,128)(2,1)S(1)}, bf16[64,1536]{1,0:T(8,128)(2,1)S(1)}, u32[]{:S(2)}, u32[]{:S(2)}) collective-permute-start(bf16[64,1536]{1,0:T(8,128)(2,1)S(1)} %get-tuple-element.240), channel_id=1, source_target_pairs={{0,16},{4,20},{8,24},{12,28},{16,32},{20,36},{24,40},{28,44},{32,4... | collective-permute-start | bytes 589832 | tf_op jit(solution)/shard_map/while/body/eval_jaxpr/ppermute | solution.py:9
  60.9 17.4 %collective-permute-start = (bf16[64,12]{1,0:T(8,128)(2,1)S(1)}, bf16[64,12]{1,0:T(8,128)(2,1)S(1)}, u32[]{:S(2)}, u32[]{:S(2)}) collective-permute-start(bf16[64,12]{1,0:T(8,128)(2,1)S(1)} %get-tuple-element.241), channel_id=1, source_target_pairs={{0,16},{4,20},{8,24},{12,28},{16,32},{20,36},{24,40},{28,44},{32,4... | collective-permute-start | bytes 4616 | tf_op jit(solution)/shard_map/while/body/eval_jaxpr/ppermute | solution.py:9
  80.0 17.0 %collective-permute-start.1 = (bf16[64,1536]{1,0:T(8,128)(2,1)S(1)}, bf16[64,1536]{1,0:T(8,128)(2,1)S(1)}, u32[]{:S(2)}, u32[]{:S(2)}) collective-permute-start(bf16[64,1536]{1,0:T(8,128)(2,1)S(1)} %get-tuple-element.240), channel_id=1, source_target_pairs={{0,16},{4,20},{8,24},{12,28},{16,32},{20,36},{24,40},{28,44},{32,4... | collective-permute-start | bytes 589832 | tf_op jit(solution)/shard_map/while/body/eval_jaxpr/ppermute | solution.py:9
  80.1 16.9 %collective-permute-start = (bf16[64,12]{1,0:T(8,128)(2,1)S(1)}, bf16[64,12]{1,0:T(8,128)(2,1)S(1)}, u32[]{:S(2)}, u32[]{:S(2)}) collective-permute-start(bf16[64,12]{1,0:T(8,128)(2,1)S(1)} %get-tuple-element.241), channel_id=1, source_target_pairs={{0,16},{4,20},{8,24},{12,28},{16,32},{20,36},{24,40},{28,44},{32,4... | collective-permute-start | bytes 4616 | tf_op jit(solution)/shard_map/while/body/eval_jaxpr/ppermute | solution.py:9
  98.7 13.2 %collective-permute-start.1 = (bf16[64,1536]{1,0:T(8,128)(2,1)S(1)}, bf16[64,1536]{1,0:T(8,128)(2,1)S(1)}, u32[]{:S(2)}, u32[]{:S(2)}) collective-permute-start(bf16[64,1536]{1,0:T(8,128)(2,1)S(1)} %get-tuple-element.240), channel_id=1, source_target_pairs={{0,16},{4,20},{8,24},{12,28},{16,32},{20,36},{24,40},{28,44},{32,4... | collective-permute-start | bytes 589832 | tf_op jit(solution)/shard_map/while/body/eval_jaxpr/ppermute | solution.py:9
  98.8 13.1 %collective-permute-start = (bf16[64,12]{1,0:T(8,128)(2,1)S(1)}, bf16[64,12]{1,0:T(8,128)(2,1)S(1)}, u32[]{:S(2)}, u32[]{:S(2)}) collective-permute-start(bf16[64,12]{1,0:T(8,128)(2,1)S(1)} %get-tuple-element.241), channel_id=1, source_target_pairs={{0,16},{4,20},{8,24},{12,28},{16,32},{20,36},{24,40},{28,44},{32,4... | collective-permute-start | bytes 4616 | tf_op jit(solution)/shard_map/while/body/eval_jaxpr/ppermute | solution.py:9
  113.6 12.3 %collective-permute-start.1 = (bf16[64,1536]{1,0:T(8,128)(2,1)S(1)}, bf16[64,1536]{1,0:T(8,128)(2,1)S(1)}, u32[]{:S(2)}, u32[]{:S(2)}) collective-permute-start(bf16[64,1536]{1,0:T(8,128)(2,1)S(1)} %get-tuple-element.240), channel_id=1, source_target_pairs={{0,16},{4,20},{8,24},{12,28},{16,32},{20,36},{24,40},{28,44},{32,4... | collective-permute-start | bytes 589832 | tf_op jit(solution)/shard_map/while/body/eval_jaxpr/ppermute | solution.py:9
  168.1 12.2 %collective-permute-start.1 = (bf16[64,1536]{1,0:T(8,128)(2,1)S(1)}, bf16[64,1536]{1,0:T(8,128)(2,1)S(1)}, u32[]{:S(2)}, u32[]{:S(2)}) collective-permute-start(bf16[64,1536]{1,0:T(8,128)(2,1)S(1)} %get-tuple-element.240), channel_id=1, source_target_pairs={{0,16},{4,20},{8,24},{12,28},{16,32},{20,36},{24,40},{28,44},{32,4... | collective-permute-start | bytes 589832 | tf_op jit(solution)/shard_map/while/body/eval_jaxpr/ppermute | solution.py:9
  209.1 13.0 %collective-permute-start.1 = (bf16[64,1536]{1,0:T(8,128)(2,1)S(1)}, bf16[64,1536]{1,0:T(8,128)(2,1)S(1)}, u32[]{:S(2)}, u32[]{:S(2)}) collective-permute-start(bf16[64,1536]{1,0:T(8,128)(2,1)S(1)} %get-tuple-element.240), channel_id=1, source_target_pairs={{0,16},{4,20},{8,24},{12,28},{16,32},{20,36},{24,40},{28,44},{32,4... | collective-permute-start | bytes 589832 | tf_op jit(solution)/shard_map/while/body/eval_jaxpr/ppermute | solution.py:9
  209.1 12.9 %collective-permute-start = (bf16[64,12]{1,0:T(8,128)(2,1)S(1)}, bf16[64,12]{1,0:T(8,128)(2,1)S(1)}, u32[]{:S(2)}, u32[]{:S(2)}) collective-permute-start(bf16[64,12]{1,0:T(8,128)(2,1)S(1)} %get-tuple-element.241), channel_id=1, source_target_pairs={{0,16},{4,20},{8,24},{12,28},{16,32},{20,36},{24,40},{28,44},{32,4... | collective-permute-start | bytes 4616 | tf_op jit(solution)/shard_map/while/body/eval_jaxpr/ppermute | solution.py:9
  223.8 14.6 %collective-permute-start.1 = (bf16[64,1536]{1,0:T(8,128)(2,1)S(1)}, bf16[64,1536]{1,0:T(8,128)(2,1)S(1)}, u32[]{:S(2)}, u32[]{:S(2)}) collective-permute-start(bf16[64,1536]{1,0:T(8,128)(2,1)S(1)} %get-tuple-element.240), channel_id=1, source_target_pairs={{0,16},{4,20},{8,24},{12,28},{16,32},{20,36},{24,40},{28,44},{32,4... | collective-permute-start | bytes 589832 | tf_op jit(solution)/shard_map/while/body/eval_jaxpr/ppermute | solution.py:9
  223.9 14.5 %collective-permute-start = (bf16[64,12]{1,0:T(8,128)(2,1)S(1)}, bf16[64,12]{1,0:T(8,128)(2,1)S(1)}, u32[]{:S(2)}, u32[]{:S(2)}) collective-permute-start(bf16[64,12]{1,0:T(8,128)(2,1)S(1)} %get-tuple-element.241), channel_id=1, source_target_pairs={{0,16},{4,20},{8,24},{12,28},{16,32},{20,36},{24,40},{28,44},{32,4... | collective-permute-start | bytes 4616 | tf_op jit(solution)/shard_map/while/body/eval_jaxpr/ppermute | solution.py:9
  240.1 14.9 %collective-permute-start.1 = (bf16[64,1536]{1,0:T(8,128)(2,1)S(1)}, bf16[64,1536]{1,0:T(8,128)(2,1)S(1)}, u32[]{:S(2)}, u32[]{:S(2)}) collective-permute-start(bf16[64,1536]{1,0:T(8,128)(2,1)S(1)} %get-tuple-element.240), channel_id=1, source_target_pairs={{0,16},{4,20},{8,24},{12,28},{16,32},{20,36},{24,40},{28,44},{32,4... | collective-permute-start | bytes 589832 | tf_op jit(solution)/shard_map/while/body/eval_jaxpr/ppermute | solution.py:9
  240.2 14.8 %collective-permute-start = (bf16[64,12]{1,0:T(8,128)(2,1)S(1)}, bf16[64,12]{1,0:T(8,128)(2,1)S(1)}, u32[]{:S(2)}, u32[]{:S(2)}) collective-permute-start(bf16[64,12]{1,0:T(8,128)(2,1)S(1)} %get-tuple-element.241), channel_id=1, source_target_pairs={{0,16},{4,20},{8,24},{12,28},{16,32},{20,36},{24,40},{28,44},{32,4... | collective-permute-start | bytes 4616 | tf_op jit(solution)/shard_map/while/body/eval_jaxpr/ppermute | solution.py:9
  256.8 16.5 %collective-permute-start.1 = (bf16[64,1536]{1,0:T(8,128)(2,1)S(1)}, bf16[64,1536]{1,0:T(8,128)(2,1)S(1)}, u32[]{:S(2)}, u32[]{:S(2)}) collective-permute-start(bf16[64,1536]{1,0:T(8,128)(2,1)S(1)} %get-tuple-element.240), channel_id=1, source_target_pairs={{0,16},{4,20},{8,24},{12,28},{16,32},{20,36},{24,40},{28,44},{32,4... | collective-permute-start | bytes 589832 | tf_op jit(solution)/shard_map/while/body/eval_jaxpr/ppermute | solution.py:9
  257.1 16.1 %collective-permute-start = (bf16[64,12]{1,0:T(8,128)(2,1)S(1)}, bf16[64,12]{1,0:T(8,128)(2,1)S(1)}, u32[]{:S(2)}, u32[]{:S(2)}) collective-permute-start(bf16[64,12]{1,0:T(8,128)(2,1)S(1)} %get-tuple-element.241), channel_id=1, source_target_pairs={{0,16},{4,20},{8,24},{12,28},{16,32},{20,36},{24,40},{28,44},{32,4... | collective-permute-start | bytes 4616 | tf_op jit(solution)/shard_map/while/body/eval_jaxpr/ppermute | solution.py:9
  274.9 16.2 %collective-permute-start.1 = (bf16[64,1536]{1,0:T(8,128)(2,1)S(1)}, bf16[64,1536]{1,0:T(8,128)(2,1)S(1)}, u32[]{:S(2)}, u32[]{:S(2)}) collective-permute-start(bf16[64,1536]{1,0:T(8,128)(2,1)S(1)} %get-tuple-element.240), channel_id=1, source_target_pairs={{0,16},{4,20},{8,24},{12,28},{16,32},{20,36},{24,40},{28,44},{32,4... | collective-permute-start | bytes 589832 | tf_op jit(solution)/shard_map/while/body/eval_jaxpr/ppermute | solution.py:9
  275.0 16.1 %collective-permute-start = (bf16[64,12]{1,0:T(8,128)(2,1)S(1)}, bf16[64,12]{1,0:T(8,128)(2,1)S(1)}, u32[]{:S(2)}, u32[]{:S(2)}) collective-permute-start(bf16[64,12]{1,0:T(8,128)(2,1)S(1)} %get-tuple-element.241), channel_id=1, source_target_pairs={{0,16},{4,20},{8,24},{12,28},{16,32},{20,36},{24,40},{28,44},{32,4... | collective-permute-start | bytes 4616 | tf_op jit(solution)/shard_map/while/body/eval_jaxpr/ppermute | solution.py:9
  (14 other events, 143.9 us)
Sparse Core Ops, SparseCore 0:
  293.7 63.0 all-reduce.1
